TPU v7x, 32 devices: a whole 2x2x4 slice. The times are simulated.
32 devices in a mesh: ctx: 8 (over y, x, core), uly: 4 (over z).
Axes of the slice: x: 2, y: 2, z: 4, core: 2. Of those that a mesh axis runs over, the one named last changes fastest.
Arguments:
- query_states: bfloat16 [1024, 2048], P(('ctx', 'uly')), may hold values from -8 to 8
- key_states: bfloat16 [1024, 2048], P(('ctx', 'uly')), may hold values from -8 to 8
- value_states: bfloat16 [1024, 2048], P(('ctx', 'uly')), may hold values from -6 to 6
- score_kernel: float32 [16, 6, 11], P('uly'), may hold values from -0.4 to 1.2
- head_mixing: float32 [16, 4], P('uly'), may hold values from 0.25 to 1
- head_gain: float32 [2048], P('uly'), may hold values from 0.5 to 1.5
Outputs:
- attended: bfloat16 [1024, 2048], P(('ctx', 'uly'))
All inputs are finite; a program needn't handle non-finite values.
Results may differ from a plain program's by a relative error of at most 0.0049.
Values may be sent and summed in bfloat16 or wider, within the bound.
No kernel may reach another device: no remote copies, remote signals or barrier semaphores. Data moves between devices by JAX's collectives and lax.ppermute only.
A program may use at most 64 MiB of HBM per device.

v0:
```python
import jax
import jax.numpy as jnp
from jax import lax
from jax.sharding import PartitionSpec as P

GROUP = 4
QCONV = 6
KCONV = 11
KEY_BLOCK = 128
ROW_CHUNK = 128
KEY_GROUP = 8
lowest = -1e30
epsilon = 1e-06


def passed_along(shard, axis, by):
    peers = lax.axis_size(axis)
    pairs = [(i, i + by) for i in range(peers) if 0 <= i + by < peers]
    return lax.ppermute(shard, axis, pairs)


def split_bf16(values):
    high = lax.reduce_precision(values, exponent_bits=8, mantissa_bits=7)
    low = values - high
    return (high.astype(jnp.bfloat16), low.astype(jnp.bfloat16))


def toeplitz_terms(score_kernel, head_dim):
    col_lead = KCONV - 1
    scaled = score_kernel * head_dim ** (-0.5)
    lag = (
        lax.iota(jnp.int32, KEY_BLOCK)[:, None]
        + col_lead
        - lax.iota(jnp.int32, KEY_BLOCK + col_lead)[None, :]
    )
    toeplitz = jnp.zeros(score_kernel.shape[:2] + lag.shape, jnp.float32)
    for col_lag in range(KCONV):
        toeplitz = jnp.where(lag == col_lag, scaled[:, :, col_lag, None, None], toeplitz)
    return split_bf16(toeplitz)


def convolved_keys(key_windows, terms):
    high, low = terms
    heads = high.shape[0]
    key_heads = key_windows.reshape(key_windows.shape[:2] + (heads, -1))
    conv_keys = jnp.einsum(
        "harc,nchd->nhard", high, key_heads, preferred_element_type=jnp.float32
    ) + jnp.einsum("harc,nchd->nhard", low, key_heads, preferred_element_type=jnp.float32)
    return split_bf16(conv_keys)


def band_terms(query_rows, query_first, key_flat, score_kernel):
    row_lead = QCONV - 1
    heads = score_kernel.shape[0]
    ext_count = query_rows.shape[0]
    row_count = ext_count - row_lead
    near = lax.dynamic_slice_in_dim(key_flat, query_first + 4, ext_count + QCONV - 2, 0)
    query_heads = query_rows.reshape(ext_count, heads, -1).astype(jnp.float32)
    near_heads = near.reshape(near.shape[0], heads, -1).astype(jnp.float32)
    scale = query_heads.shape[2] ** (-0.5)
    diagonals = [
        jnp.sum(query_heads * near_heads[lag - 1 : lag - 1 + ext_count], axis=2) * scale
        for lag in range(1, QCONV)
    ]
    band = []
    for gap in range(QCONV - 1):
        acc = jnp.zeros((row_count, heads), jnp.float32)
        for row_lag in range(gap + 1, QCONV):
            for col_lag in range(row_lag - gap):
                lag = row_lag - col_lag - gap
                acc = (
                    acc
                    - score_kernel[None, :, row_lag, col_lag]
                    * diagonals[lag - 1][row_lead - row_lag : row_lead - row_lag + row_count]
                )
        band.append(acc.T)
    return jnp.stack(band)


def group_logits(shifted, key_windows, terms):
    keys_high, keys_low = convolved_keys(key_windows, terms)
    return jnp.einsum(
        "ihad,nhard->hinr", shifted, keys_high, preferred_element_type=jnp.float32
    ) + jnp.einsum("ihad,nhard->hinr", shifted, keys_low, preferred_element_type=jnp.float32)


def attend_chunk(shifted, band, query_first, key_windows, terms, value_heads, head_mixing):
    row_count, heads = shifted.shape[:2]
    seq_len = value_heads.shape[0]
    window_count = key_windows.shape[0]
    if window_count <= KEY_GROUP:
        convolved = group_logits(shifted, key_windows, terms)
    else:
        grouped_windows = key_windows.reshape(
            (window_count // KEY_GROUP, KEY_GROUP) + key_windows.shape[1:]
        )
        convolved = lax.map(lambda windows: group_logits(shifted, windows, terms), grouped_windows)
        convolved = jnp.moveaxis(convolved, 0, 2)
    convolved = convolved.reshape(heads, row_count, seq_len)
    query_pos = query_first + lax.iota(jnp.int32, row_count)
    gap = query_pos[:, None] - lax.iota(jnp.int32, seq_len)[None, :]
    for lag in range(QCONV - 1):
        convolved = convolved + jnp.where(gap == lag, band[lag][:, :, None], 0.0)
    logits = jnp.where(gap >= 0, convolved, lowest)
    peak = jnp.max(logits, axis=2, keepdims=True)
    expd = jnp.exp(logits - peak)
    probabilities = expd / jnp.sum(expd, axis=2, keepdims=True)
    grouped = probabilities.reshape(heads // GROUP, GROUP, row_count, seq_len)
    weights = head_mixing.reshape(heads // GROUP, GROUP, GROUP)
    mixed_probs = jnp.zeros_like(grouped)
    for source in range(GROUP):
        mixed_probs = mixed_probs + weights[:, :, source, None, None] * grouped[:, source, None]
    mixed_probs = mixed_probs.reshape(heads, row_count, seq_len).astype(jnp.bfloat16)
    return jnp.einsum("hik,khd->ihd", mixed_probs, value_heads, preferred_element_type=jnp.float32)


def normalize(weighted, gain_local):
    factor = lax.rsqrt(jnp.mean(weighted * weighted, axis=2, keepdims=True) + epsilon)
    return (
        (weighted * factor * gain_local[None]).astype(jnp.bfloat16).reshape(weighted.shape[0], -1)
    )


def shards(query_states, key_states, value_states, score_kernel, head_mixing, head_gain):
    stacked = jnp.stack([query_states, key_states, value_states])
    query_local, key_local, value_local = lax.all_to_all(
        stacked, "uly", split_axis=2, concat_axis=1, tiled=True
    )
    shard_rows = query_local.shape[0]
    width = query_local.shape[1]
    row_lead = QCONV - 1
    col_lead = KCONV - 1
    heads = score_kernel.shape[0]
    head_dim = width // heads
    ctx_place = lax.axis_index("ctx")
    query_first = ctx_place * shard_rows
    earlier = passed_along(query_local[shard_rows - row_lead :], "ctx", 1)
    query_ext = jnp.concatenate([earlier, query_local], axis=0)
    key_all, value_all = lax.all_gather(
        jnp.stack([key_local, value_local]), "ctx", axis=1, tiled=True
    )
    seq_len = key_all.shape[0]
    key_pad = jnp.concatenate([jnp.zeros((col_lead, width), key_all.dtype), key_all], axis=0)
    key_windows = jnp.stack(
        [key_pad[start : start + KEY_BLOCK + col_lead] for start in range(0, seq_len, KEY_BLOCK)]
    )
    terms = toeplitz_terms(score_kernel, head_dim)
    edge = jnp.zeros((8, width), key_all.dtype)
    key_flat = jnp.concatenate([edge, key_all, edge], axis=0)
    band = band_terms(query_ext, query_first, key_flat, score_kernel)
    query_heads = query_ext.reshape(shard_rows + row_lead, heads, head_dim)
    shifted = jnp.stack(
        [query_heads[row_lead - lag : row_lead - lag + shard_rows] for lag in range(QCONV)], axis=2
    )
    value_heads = value_all.reshape(seq_len, heads, head_dim)
    chunk = min(ROW_CHUNK * KEY_BLOCK * 8 // seq_len, shard_rows)
    if chunk == shard_rows:
        weighted = attend_chunk(
            shifted, band, query_first, key_windows, terms, value_heads, head_mixing
        )
    else:
        chunks = shard_rows // chunk

        def one_chunk(index):
            start = index * chunk
            return attend_chunk(
                lax.dynamic_slice_in_dim(shifted, start, chunk, 0),
                lax.dynamic_slice_in_dim(band, start, chunk, 2),
                query_first + start,
                key_windows,
                terms,
                value_heads,
                head_mixing,
            )

        weighted = lax.map(one_chunk, jnp.arange(chunks, dtype=jnp.int32))
        weighted = weighted.reshape((shard_rows,) + weighted.shape[2:])
    gain_local = head_gain.reshape(heads, head_dim)
    attended = normalize(weighted, gain_local)
    return lax.all_to_all(attended, "uly", split_axis=0, concat_axis=1, tiled=True)


def solution(mesh):
    placed = (
        P(("ctx", "uly"), None),
        P(("ctx", "uly"), None),
        P(("ctx", "uly"), None),
        P("uly", None, None),
        P("uly", None),
        P("uly"),
    )
    return jax.shard_map(
        shards, mesh=mesh, in_specs=placed, out_specs=P(("ctx", "uly"), None), check_vma=False
    )
```

profile of v0, /device:TPU:0, one launch (start us, length us, event | category | flops | bytes accessed | tf_op | source)
XLA Modules:
  0.0 156.9 jit_solution(3671239521716522393)
XLA Ops:
  6.5 1.1 pad_maximum_fusion
  7.6 1.4 copy.223
  9.0 1.6 %reshape.295 = bf16[4,2,24576]{2,1,0:T(2,128)(2,1)S(1)} reshape(bf16[2048,3,32]{2,1,0:T(4,128)(2,1)S(1)} %bitcast.118) | data formatting | bytes 786432
  10.6 17.8 %all_to_all.34 = bf16[4,2,24576]{2,1,0:T(2,128)(2,1)S(1)} all-to-all(bf16[4,2,24576]{2,1,0:T(2,128)(2,1)S(1)} %reshape.295), channel_id=1, replica_groups=mesh['ctx'=8,'uly'=4] {'uly'}, dimensions={0} | all-to-all | bytes 786432 | tf_op jit(solution)/shard_map/all_to_all | solution.py:126
  28.4 1.3 reshape.296
  29.7 1.2 copy.282
  30.9 0.1 fusion.128
  31.1 0.8 pad_maximum_fusion.1
  32.5 0.7 copy.255
  33.2 0.6 copy.254
  33.8 0.7 copy.253
  34.5 0.7 copy.252
  35.2 0.7 copy.251
  35.9 0.7 copy.250
  36.5 0.7 copy.249
  37.2 0.7 slice_reduce_fusion.18
  38.0 1.0 slice_reduce_fusion.17
  39.0 0.8 fusion.108
  39.7 1.2 fusion.84
  41.0 1.2 subtract_compare_fusion.5
  42.3 1.3 collective-permute-start
  43.6 0.7 concatenate.20
  45.2 0.1 copy.238
  45.7 0.1 copy.240
  45.8 0.6 concatenate.19
  46.6 12.5 %all-gather.2.cloned.1.call-done = bf16[2,1024,512]{2,1,0:T(8,128)(2,1)} async-done(((bf16[2,128,512]{2,1,0:T(8,128)(2,1)}), bf16[2,1024,512]{2,1,0:T(8,128)(2,1)}) %all-gather.2.cloned.1.call-update) | async-done | bytes 2097168 | tf_op jit(solution)/shard_map/all_gather | solution.py:139
  59.1 1.7 %slice_bitcast_fusion = (bf16[1024,512]{1,0:T(8,128)(2,1)S(1)}, bf16[1,1024,512]{2,1,0:T(8,128)(2,1)S(1)}) fusion(bf16[2,1024,512]{2,1,0:T(8,128)(2,1)} %all-gather.2.cloned.1.call-done), kind=kLoop, calls=%fused_computation.39 | loop fusion | bytes 4194304 | tf_op jit(solution)/shard_map/unstack | solution.py:139
  60.8 0.7 pad_slice_fusion
  61.5 1.6 %stack.75 = bf16[1,138,4,128]{3,2,1,0:T(4,128)(2,1)} reshape(bf16[138,512]{1,0:T(8,128)(2,1)} %pad_slice_fusion) | data formatting | bytes 282624 | tf_op jit(solution)/shard_map/stack | solution.py:144
  63.1 1.6 %copy_dynamic-update-slice_fusion.7 = bf16[8,138,4,128]{3,1,0,2:T(8,128)(2,1)} fusion(bf16[1,138,4,128]{3,2,1,0:T(4,128)(2,1)} %stack.75), kind=kLoop, calls=%fused_computation.138 | loop fusion | bytes 288768
  64.7 2.4 %fusion.127 = (bf16[1,138,512]{2,1,0:T(8,128)(2,1)}, bf16[1,138,512]{2,1,0:T(8,128)(2,1)}, bf16[1,138,512]{2,1,0:T(8,128)(2,1)}, bf16[1,138,512]{2,1,0:T(8,128)(...) fusion(bf16[2,1024,512]{2,1,0:T(8,128)(2,1)} %all-gather.2.cloned.1.call-done), kind=kLoop, calls=%fused_computation.217 | loop fusion | bytes 1978368 | tf_op jit(solution)/shard_map/slice | solution.py:145
  67.1 1.6 %stack.76 = bf16[1,138,4,128]{3,2,1,0:T(4,128)(2,1)} reshape(bf16[1,138,512]{2,1,0:T(8,128)(2,1)} %get-tuple-element.39) | data formatting | bytes 282624 | tf_op jit(solution)/shard_map/stack | solution.py:144
  68.7 1.6 %stack.77 = bf16[1,138,4,128]{3,2,1,0:T(4,128)(2,1)} reshape(bf16[1,138,512]{2,1,0:T(8,128)(2,1)} %get-tuple-element.38) | data formatting | bytes 282624 | tf_op jit(solution)/shard_map/stack | solution.py:144
  70.3 1.6 %stack.78 = bf16[1,138,4,128]{3,2,1,0:T(4,128)(2,1)} reshape(bf16[1,138,512]{2,1,0:T(8,128)(2,1)} %get-tuple-element.37) | data formatting | bytes 282624 | tf_op jit(solution)/shard_map/stack | solution.py:144
  71.9 1.6 %stack.79 = bf16[1,138,4,128]{3,2,1,0:T(4,128)(2,1)} reshape(bf16[1,138,512]{2,1,0:T(8,128)(2,1)} %get-tuple-element.36) | data formatting | bytes 282624 | tf_op jit(solution)/shard_map/stack | solution.py:144
  73.5 1.6 %stack.80 = bf16[1,138,4,128]{3,2,1,0:T(4,128)(2,1)} reshape(bf16[1,138,512]{2,1,0:T(8,128)(2,1)} %get-tuple-element.35) | data formatting | bytes 282624 | tf_op jit(solution)/shard_map/stack | solution.py:144
  75.1 1.6 %stack.81 = bf16[1,138,4,128]{3,2,1,0:T(4,128)(2,1)} reshape(bf16[1,138,512]{2,1,0:T(8,128)(2,1)} %get-tuple-element.34) | data formatting | bytes 282624 | tf_op jit(solution)/shard_map/stack | solution.py:144
  76.7 1.6 %stack.82 = bf16[1,138,4,128]{3,2,1,0:T(4,128)(2,1)} reshape(bf16[1,138,512]{2,1,0:T(8,128)(2,1)} %get-tuple-element.33) | data formatting | bytes 282624 | tf_op jit(solution)/shard_map/stack | solution.py:144
  78.3 1.6 %copy_dynamic-update-slice_fusion.6 = bf16[8,138,4,128]{3,1,0,2:T(8,128)(2,1)} fusion(bf16[8,138,4,128]{3,1,0,2:T(8,128)(2,1)} %copy_dynamic-update-slice_fusion.7, bf16[1,138,4,128]{3,2,1,0:T(4,128)(2,1)} %stack.76), kind=kLoop, calls=%fused_computation.137 | loop fusion | bytes 288768
  79.9 1.6 %copy_dynamic-update-slice_fusion.5 = bf16[8,138,4,128]{3,1,0,2:T(8,128)(2,1)} fusion(bf16[8,138,4,128]{3,1,0,2:T(8,128)(2,1)} %copy_dynamic-update-slice_fusion.6, bf16[1,138,4,128]{3,2,1,0:T(4,128)(2,1)} %stack.77), kind=kLoop, calls=%fused_computation.136 | loop fusion | bytes 288768
  81.5 1.6 %copy_dynamic-update-slice_fusion.4 = bf16[8,138,4,128]{3,1,0,2:T(8,128)(2,1)} fusion(bf16[8,138,4,128]{3,1,0,2:T(8,128)(2,1)} %copy_dynamic-update-slice_fusion.5, bf16[1,138,4,128]{3,2,1,0:T(4,128)(2,1)} %stack.78), kind=kLoop, calls=%fused_computation.135 | loop fusion | bytes 288768
  83.1 1.6 %copy_dynamic-update-slice_fusion.3 = bf16[8,138,4,128]{3,1,0,2:T(8,128)(2,1)} fusion(bf16[8,138,4,128]{3,1,0,2:T(8,128)(2,1)} %copy_dynamic-update-slice_fusion.4, bf16[1,138,4,128]{3,2,1,0:T(4,128)(2,1)} %stack.79), kind=kLoop, calls=%fused_computation.134 | loop fusion | bytes 288768
  84.7 1.6 %copy_dynamic-update-slice_fusion.2 = bf16[8,138,4,128]{3,1,0,2:T(8,128)(2,1)} fusion(bf16[8,138,4,128]{3,1,0,2:T(8,128)(2,1)} %copy_dynamic-update-slice_fusion.3, bf16[1,138,4,128]{3,2,1,0:T(4,128)(2,1)} %stack.80), kind=kLoop, calls=%fused_computation.133 | loop fusion | bytes 288768
  86.3 1.6 %copy_dynamic-update-slice_fusion.1 = bf16[8,138,4,128]{3,1,0,2:T(8,128)(2,1)} fusion(bf16[8,138,4,128]{3,1,0,2:T(8,128)(2,1)} %copy_dynamic-update-slice_fusion.2, bf16[1,138,4,128]{3,2,1,0:T(4,128)(2,1)} %stack.81), kind=kLoop, calls=%fused_computation.132 | loop fusion | bytes 288768
  87.9 1.6 %copy_dynamic-update-slice_fusion = bf16[8,138,4,128]{3,1,0,2:T(8,128)(2,1)} fusion(bf16[8,138,4,128]{3,1,0,2:T(8,128)(2,1)} %copy_dynamic-update-slice_fusion.1, bf16[1,138,4,128]{3,2,1,0:T(4,128)(2,1)} %stack.82), kind=kLoop, calls=%fused_computation.131 | loop fusion | bytes 288768 | tf_op jit(solution)/shard_map/stack | solution.py:144
  89.6 8.7 %fusion.17 = f32[4,8,128,6,128]{4,2,3,1,0:T(8,128)} fusion(bf16[8,138,4,128]{3,1,0,2:T(8,128)(2,1)} %copy_dynamic-update-slice_fusion, f32[4,6]{1,0:T(4,128)S(1)} %bitcast.135, f32[4,6]{1,0:T(4,128)S(1)} %bitcast.137, f32[4,6]{1,0:T(4,128)S(1)} %bitcast.139, f32[4,6]{1,0:T(4,128)S(1)} %bitcast.141, f32[4,6]{1,0:T(4,128)} %bitcast.143, ...), kind=kOutput, calls=%fused_computation.32 | convolution fusion | flops 873732096 | bytes 13908768 | tf_op jit(solution)/shard_map/harc,nchd->nhard/dot_general | solution.py:46
  98.5 6.3 %fusion.15 = f32[4,8,128,6,128]{4,2,3,1,0:T(8,128)} fusion(bf16[8,138,4,128]{3,1,0,2:T(8,128)(2,1)S(1)} %copy-done, f32[4,6]{1,0:T(4,128)S(1)} %bitcast.136, f32[4,6]{1,0:T(4,128)S(1)} %bitcast.138, f32[4,6]{1,0:T(4,128)S(1)} %bitcast.140, f32[4,6]{1,0:T(4,128)S(1)} %bitcast.142, f32[4,6]{1,0:T(4,128)S(1)} %bitcast.144, f32[4,6]{1,0:T(4,128)S(1)} %bitcast.146, ...), kind=kOutput, calls=%fused_computation.30 | convolution fusion | flops 874156032 | bytes 13908768 | tf_op jit(solution)/shard_map/harc,nchd->nhard/dot_general | solution.py:48
  104.8 1.4 copy.227
  106.3 0.1 fusion.129
  107.0 0.2 copy-done.5
  107.2 0.8 fusion.90
  108.6 10.9 %fusion.1 = f32[4,128,8,128,1]{1,3,4,2,0:T(8,128)S(1)} fusion(f32[4,8,128,6,128]{4,2,3,1,0:T(8,128)} %fusion.17, f32[4,8,128,6,128]{4,2,3,1,0:T(8,128)} %fusion.15, bf16[128,4,6,128]{3,0,2,1:T(8,128)(2,1)S(1)} %constant_dynamic-update-slice_fusion), kind=kOutput, calls=%fused_computation.3 | convolution fusion | flops 817889280 | bytes 28049408 | tf_op jit(solution)/shard_map/ihad,nhard->hinr/dot_general | solution.py:84
  119.9 10.4 %fusion.85 = (f32[4,128]{1,0:T(4,128)S(1)}, f32[4,128,8,128]{1,3,2,0:T(8,128)S(1)}) fusion(f32[4,128]{1,0:T(4,128)S(1)} %get-tuple-element.74, pred[128,8,128]{0,2,1:T(8,128)(4,1)S(1)} %get-tuple-element.69, f32[4,128]{1,0:T(4,128)S(1)} %get-tuple-element.67, pred[128,8,128]{0,2,1:T(8,128)(4,1)S(1)} %get-tuple-element.70, ...), kind=kOutput, calls=%fused_computation.115 | convolution fusion | flops 821558784 | bytes 30945280 | tf_op jit(solution)/shard_map/ihad,nhard->hinr/dot_general | solution.py:82
  130.4 1.3 exponential_reduce_fusion
  131.7 1.3 fusion.13
  133.0 0.1 slice_bitcast_fusion.4
  133.1 1.0 copy.271
  134.1 1.0 copy.270
  135.2 1.0 copy.269
  136.2 0.2 copy.268
  136.5 1.8 %multiply_reduce_fusion = (f32[128,4]{0,1:T(4,128)S(1)}, f32[128,4,128]{0,2,1:T(8,128)S(1)}) fusion(bf16[1024,4,128]{0,2,1:T(8,128)(2,1)S(1)} %bitcast.123, f32[128,1024]{1,0:T(8,128)S(1)} %copy-done.3, f32[4]{0:T(128)S(1)} %copy-done.50, f32[128,1024]{1,0:T(8,128)S(1)} %copy-done.4, f32[4]{0:T(128)S(1)} %copy-done.51, f32[128,1024]{1,0:T(8,128)} %copy.269, ...), kind=kOutput, calls=%fused_computation.127 | convolution fusion | flops 138542592 | bytes 3409984 | tf_op jit(solution)/shard_map/hik,khd->ihd/dot_general | solution.py:114
  138.5 0.1 copy.272
  138.7 10.7 %all_to_all.35 = bf16[4,32,512]{2,1,0:T(8,128)(2,1)S(1)} all-to-all(bf16[4,32,512]{2,1,0:T(8,128)(2,1)S(1)} %all_to_all.28), channel_id=1, replica_groups=mesh['ctx'=8,'uly'=4] {'uly'}, dimensions={0} | all-to-all | bytes 262144 | tf_op jit(solution)/shard_map/all_to_all | solution.py:180
  149.4 0.7 copy.284
  (158 shorter events, 3.8 us)
Async XLA Ops:
  6.5 52.5 %all-gather.2.cloned.1.call-start = ((), (), s32[]{:S(2)}) async-start(), calls=%async_computation.2 | async-start | bytes 2359296 | tf_op jit(solution)/shard_map/all_gather | solution.py:139
  29.7 2.2 %copy-start.23 = (f32[4,6,11]{2,0,1:T(4,128)S(1)}, f32[4,6,11]{2,0,1:T(4,128)}, u32[]{:S(2)}) copy-start(f32[4,6,11]{2,0,1:T(4,128)} %param.9) | copy-start | bytes 3172
  29.7 7.5 %copy-start.31 = (f32[4,4]{1,0:T(4,128)S(1)}, f32[4,4]{1,0:T(4,128)}, u32[]{:S(2)}) copy-start(f32[4,4]{1,0:T(4,128)} %param.10) | copy-start | bytes 196
  42.3 2.1 %collective-permute-start = (bf16[5,512]{1,0:T(8,128)(2,1)S(1)}, bf16[5,512]{1,0:T(8,128)(2,1)S(1)}, u32[]{:S(2)}, u32[]{:S(2)}) collective-permute-start(bf16[5,512]{1,0:T(8,128)(2,1)S(1)} %slice.356), channel_id=1, source_target_pairs={{0,4},{4,8},{8,12},{12,16},{16,20},{20,24},{24,28},{1,5},{5,9},{9,... | collective-permute-start | bytes 15368 | tf_op jit(solution)/shard_map/ppermute | solution.py:19
  89.5 8.9 %copy-start = (bf16[8,138,4,128]{3,1,0,2:T(8,128)(2,1)S(1)}, bf16[8,138,4,128]{3,1,0,2:T(8,128)(2,1)}, u32[]{:S(2)}) copy-start(bf16[8,138,4,128]{3,1,0,2:T(8,128)(2,1)} %copy_dynamic-update-slice_fusion) | copy-start | bytes 3391492
  89.5 8.9 %copy-start.12 = (pred[128,138]{0,1:T(8,128)(4,1)S(1)}, pred[128,138]{0,1:T(8,128)(4,1)}, u32[]{:S(2)}) copy-start(pred[128,138]{0,1:T(8,128)(4,1)} %get-tuple-element.81) | copy-start | bytes 52996
  89.5 8.9 %copy-start.13 = (pred[128,138]{0,1:T(8,128)(4,1)S(1)}, pred[128,138]{0,1:T(8,128)(4,1)}, u32[]{:S(2)}) copy-start(pred[128,138]{0,1:T(8,128)(4,1)} %get-tuple-element.82) | copy-start | bytes 52996
  89.5 8.9 %copy-start.14 = (pred[128,138]{0,1:T(8,128)(4,1)S(1)}, pred[128,138]{0,1:T(8,128)(4,1)}, u32[]{:S(2)}) copy-start(pred[128,138]{0,1:T(8,128)(4,1)} %get-tuple-element.83) | copy-start | bytes 52996
  89.5 8.9 %copy-start.15 = (pred[128,138]{0,1:T(8,128)(4,1)S(1)}, pred[128,138]{0,1:T(8,128)(4,1)}, u32[]{:S(2)}) copy-start(pred[128,138]{0,1:T(8,128)(4,1)} %get-tuple-element.84) | copy-start | bytes 52996
  89.5 8.9 %copy-start.16 = (pred[128,138]{0,1:T(8,128)(4,1)S(1)}, pred[128,138]{0,1:T(8,128)(4,1)}, u32[]{:S(2)}) copy-start(pred[128,138]{0,1:T(8,128)(4,1)} %get-tuple-element.85) | copy-start | bytes 52996
  89.5 8.9 %copy-start.17 = (pred[128,138]{0,1:T(8,128)(4,1)S(1)}, pred[128,138]{0,1:T(8,128)(4,1)}, u32[]{:S(2)}) copy-start(pred[128,138]{0,1:T(8,128)(4,1)} %get-tuple-element.86) | copy-start | bytes 52996
  89.5 8.9 %copy-start.18 = (pred[128,138]{0,1:T(8,128)(4,1)S(1)}, pred[128,138]{0,1:T(8,128)(4,1)}, u32[]{:S(2)}) copy-start(pred[128,138]{0,1:T(8,128)(4,1)} %get-tuple-element.87) | copy-start | bytes 52996
  89.5 8.9 %copy-start.19 = (pred[128,138]{0,1:T(8,128)(4,1)S(1)}, pred[128,138]{0,1:T(8,128)(4,1)}, u32[]{:S(2)}) copy-start(pred[128,138]{0,1:T(8,128)(4,1)} %get-tuple-element.88) | copy-start | bytes 52996
  89.5 8.9 %copy-start.20 = (pred[128,138]{0,1:T(8,128)(4,1)S(1)}, pred[128,138]{0,1:T(8,128)(4,1)}, u32[]{:S(2)}) copy-start(pred[128,138]{0,1:T(8,128)(4,1)} %get-tuple-element.89) | copy-start | bytes 52996
  89.5 8.9 %copy-start.21 = (pred[128,138]{0,1:T(8,128)(4,1)S(1)}, pred[128,138]{0,1:T(8,128)(4,1)}, u32[]{:S(2)}) copy-start(pred[128,138]{0,1:T(8,128)(4,1)} %get-tuple-element.90) | copy-start | bytes 52996
  89.6 8.9 %copy-start.22 = (pred[128,138]{0,1:T(8,128)(4,1)S(1)}, pred[128,138]{0,1:T(8,128)(4,1)}, u32[]{:S(2)}) copy-start(pred[128,138]{0,1:T(8,128)(4,1)} %get-tuple-element.91) | copy-start | bytes 52996
  89.6 8.9 %copy-start.24 = (f32[4,6,1]{1,0,2:T(4,128)S(1)}, f32[4,6,1]{1,0,2:T(4,128)}, u32[]{:S(2)}) copy-start(f32[4,6,1]{1,0,2:T(4,128)} %copy.255) | copy-start | bytes 292
  89.6 8.9 %copy-start.25 = (f32[4,6,1]{1,0,2:T(4,128)S(1)}, f32[4,6,1]{1,0,2:T(4,128)}, u32[]{:S(2)}) copy-start(f32[4,6,1]{1,0,2:T(4,128)} %copy.254) | copy-start | bytes 292
  89.6 8.9 %copy-start.26 = (f32[4,6,1]{1,0,2:T(4,128)S(1)}, f32[4,6,1]{1,0,2:T(4,128)}, u32[]{:S(2)}) copy-start(f32[4,6,1]{1,0,2:T(4,128)} %copy.253) | copy-start | bytes 292
  89.6 8.9 %copy-start.27 = (f32[4,6,1]{1,0,2:T(4,128)S(1)}, f32[4,6,1]{1,0,2:T(4,128)}, u32[]{:S(2)}) copy-start(f32[4,6,1]{1,0,2:T(4,128)} %copy.252) | copy-start | bytes 292
  89.6 8.9 %copy-start.28 = (f32[4,6,1]{1,0,2:T(4,128)S(1)}, f32[4,6,1]{1,0,2:T(4,128)}, u32[]{:S(2)}) copy-start(f32[4,6,1]{1,0,2:T(4,128)} %copy.251) | copy-start | bytes 292
  89.6 8.9 %copy-start.29 = (f32[4,6,1]{1,0,2:T(4,128)S(1)}, f32[4,6,1]{1,0,2:T(4,128)}, u32[]{:S(2)}) copy-start(f32[4,6,1]{1,0,2:T(4,128)} %copy.250) | copy-start | bytes 292
  89.6 8.9 %copy-start.30 = (f32[4,6,1]{1,0,2:T(4,128)S(1)}, f32[4,6,1]{1,0,2:T(4,128)}, u32[]{:S(2)}) copy-start(f32[4,6,1]{1,0,2:T(4,128)} %copy.249) | copy-start | bytes 292
  106.3 0.9 copy-start.5
  106.3 0.9 copy-start.32
  108.4 11.0 %copy-start.33 = (f32[4]{0:T(128)S(1)}, f32[4]{0:T(128)}, u32[]{:S(2)}) copy-start(f32[4]{0:T(128)} %get-tuple-element.11) | copy-start | bytes 52
  108.4 11.0 %copy-start.34 = (f32[4]{0:T(128)S(1)}, f32[4]{0:T(128)}, u32[]{:S(2)}) copy-start(f32[4]{0:T(128)} %get-tuple-element.12) | copy-start | bytes 52
  108.4 11.0 %copy-start.35 = (f32[4]{0:T(128)S(1)}, f32[4]{0:T(128)}, u32[]{:S(2)}) copy-start(f32[4]{0:T(128)} %get-tuple-element.13) | copy-start | bytes 52
  108.5 11.0 %copy-start.36 = (f32[4]{0:T(128)S(1)}, f32[4]{0:T(128)}, u32[]{:S(2)}) copy-start(f32[4]{0:T(128)} %get-tuple-element.16) | copy-start | bytes 52
  108.5 11.0 %copy-start.37 = (f32[4]{0:T(128)S(1)}, f32[4]{0:T(128)}, u32[]{:S(2)}) copy-start(f32[4]{0:T(128)} %get-tuple-element.17) | copy-start | bytes 52
  108.5 11.0 %copy-start.38 = (f32[4]{0:T(128)S(1)}, f32[4]{0:T(128)}, u32[]{:S(2)}) copy-start(f32[4]{0:T(128)} %get-tuple-element.20) | copy-start | bytes 52
  108.5 11.1 %copy-start.39 = (f32[4]{0:T(128)S(1)}, f32[4]{0:T(128)}, u32[]{:S(2)}) copy-start(f32[4]{0:T(128)} %get-tuple-element.15) | copy-start | bytes 52
  108.5 11.1 %copy-start.40 = (f32[4]{0:T(128)S(1)}, f32[4]{0:T(128)}, u32[]{:S(2)}) copy-start(f32[4]{0:T(128)} %get-tuple-element.19) | copy-start | bytes 52
  108.5 11.1 %copy-start.41 = (f32[4]{0:T(128)S(1)}, f32[4]{0:T(128)}, u32[]{:S(2)}) copy-start(f32[4]{0:T(128)} %get-tuple-element.22) | copy-start | bytes 52
  108.5 11.1 %copy-start.42 = (f32[4]{0:T(128)S(1)}, f32[4]{0:T(128)}, u32[]{:S(2)}) copy-start(f32[4]{0:T(128)} %get-tuple-element.24) | copy-start | bytes 52
  108.5 11.2 %copy-start.44 = (f32[4]{0:T(128)S(1)}, f32[4]{0:T(128)}, u32[]{:S(2)}) copy-start(f32[4]{0:T(128)} %get-tuple-element.10) | copy-start | bytes 52
  108.5 11.2 %copy-start.45 = (f32[4]{0:T(128)S(1)}, f32[4]{0:T(128)}, u32[]{:S(2)}) copy-start(f32[4]{0:T(128)} %get-tuple-element.14) | copy-start | bytes 52
  108.5 11.2 %copy-start.46 = (f32[4]{0:T(128)S(1)}, f32[4]{0:T(128)}, u32[]{:S(2)}) copy-start(f32[4]{0:T(128)} %get-tuple-element.18) | copy-start | bytes 52
  108.6 11.2 %copy-start.47 = (f32[4]{0:T(128)S(1)}, f32[4]{0:T(128)}, u32[]{:S(2)}) copy-start(f32[4]{0:T(128)} %get-tuple-element.21) | copy-start | bytes 52
  108.6 11.2 %copy-start.48 = (f32[4]{0:T(128)S(1)}, f32[4]{0:T(128)}, u32[]{:S(2)}) copy-start(f32[4]{0:T(128)} %get-tuple-element.23) | copy-start | bytes 52
  108.6 11.3 %copy-start.1 = (pred[128,8,128]{0,2,1:T(8,128)(4,1)S(1)}, pred[128,8,128]{0,2,1:T(8,128)(4,1)}, u32[]{:S(2)}) copy-start(pred[128,8,128]{0,2,1:T(8,128)(4,1)} %get-tuple-element.73) | copy-start | bytes 393220
  130.3 1.3 copy-start.6
  130.3 1.3 copy-start.7
  130.3 1.3 copy-start.8
  130.4 1.3 copy-start.9
  130.4 1.3 copy-start.10
  130.4 1.3 copy-start.11
  133.1 3.3 %copy-start.2 = (bf16[1,1024,512]{1,2,0:T(8,128)(2,1)S(1)}, bf16[1,1024,512]{1,2,0:T(8,128)(2,1)}, u32[]{:S(2)}) copy-start(bf16[1,1024,512]{1,2,0:T(8,128)(2,1)} %copy.227) | copy-start | bytes 3145732
  133.1 3.3 %copy-start.49 = (f32[4]{0:T(128)S(1)}, f32[4]{0:T(128)}, u32[]{:S(2)}) copy-start(f32[4]{0:T(128)} %get-tuple-element.25) | copy-start | bytes 52
  133.1 3.3 %copy-start.50 = (f32[4]{0:T(128)S(1)}, f32[4]{0:T(128)}, u32[]{:S(2)}) copy-start(f32[4]{0:T(128)} %get-tuple-element.26) | copy-start | bytes 52
  133.1 3.3 %copy-start.51 = (f32[4]{0:T(128)S(1)}, f32[4]{0:T(128)}, u32[]{:S(2)}) copy-start(f32[4]{0:T(128)} %get-tuple-element.27) | copy-start | bytes 52
  133.1 3.3 %copy-start.52 = (f32[4]{0:T(128)S(1)}, f32[4]{0:T(128)}, u32[]{:S(2)}) copy-start(f32[4]{0:T(128)} %get-tuple-element.28) | copy-start | bytes 52
  134.1 2.3 %copy-start.3 = (f32[128,1024]{1,0:T(8,128)S(1)}, f32[128,1024]{1,0:T(8,128)}, u32[]{:S(2)}) copy-start(f32[128,1024]{1,0:T(8,128)} %copy.271) | copy-start | bytes 1572868
  135.2 1.3 copy-start.4
  136.4 1.9 %copy-start.43 = (f32[512]{0:T(512)S(1)}, f32[512]{0:T(512)}, u32[]{:S(2)}) copy-start(f32[512]{0:T(512)} %param.11) | copy-start | bytes 6148
Sparse Core Ops, SparseCore 0:
  32.0 26.9 all-gather.1
where the time goes:
time: 158 us; the launch traced here: 157 us
  local copies, waits for them, and re-layouts  52.8 us (33%)
  matrix products  38.1 us (24%)
  blocking collectives  28.5 us (18%)
  between operations  14.5 us (9%)
  waiting for transfers between devices  12.6 us (8%)
  other arithmetic  9 us (6%)
    all_to_all x1, blocking collectives, shards(): lax.all_to_all(stacked, 'uly', split_axis=2, concat_axis=1, tiled=True)  17.8 us
    unnamed x121, local copies, waits for them, and re-layouts  14.7 us
    another operation x9, local copies, waits for them, and re-layouts, shards(): jnp.stack([key_pad[start:start + KEY_BLOCK + col_lead] for start in range...  14.4 us
    all_gather x1, waiting for transfers between devices, shards(): lax.all_gather(jnp.stack([key_local, value_local]), 'ctx', axis=1, tiled=...  12.5 us
    dot_general x1, matrix products, group_logits(): jnp.einsum('ihad,nhard->hinr', shifted, keys_low, preferred_element_type=...  10.9 us
    all_to_all x1, blocking collectives, shards(): lax.all_to_all(attended, 'uly', split_axis=0, concat_axis=1, tiled=True)  10.7 us
    dot_general x1, matrix products, group_logits(): jnp.einsum('ihad,nhard->hinr', shifted, keys_high, preferred_element_type...  10.4 us
    dot_general x1, matrix products, convolved_keys(): jnp.einsum('harc,nchd->nhard', high, key_heads, preferred_element_type=jn...  8.7 us
  transfers between devices with their start and end apart: 2, of which 2 were waited for; matrix products, arithmetic and copies ran while one was open for 8% of the time, Pallas kernels for 0%

commit v1 on v0

--- a/solution.py
+++ b/solution.py
@@ -11,6 +11,19 @@
 KEY_GROUP = 8
 lowest = -1e30
 epsilon = 1e-06
+
+
+def ring_gather(x, axis, dim):
+    ways = lax.axis_size(axis)
+    up = [(d, (d + 1) % ways) for d in range(ways)]
+    down = [(d, (d - 1) % ways) for d in range(ways)]
+    earlier, later = ([x], [x])
+    for _ in range(ways // 2):
+        earlier.append(lax.ppermute(earlier[-1], axis, up))
+    for _ in range((ways - 1) // 2):
+        later.append(lax.ppermute(later[-1], axis, down))
+    line = jnp.concatenate([*earlier[::-1], *later[1:]], axis=dim)
+    return jnp.roll(line, (lax.axis_index(axis) - ways // 2) * x.shape[dim], axis=dim)
 
 
 def passed_along(shard, axis, by):
@@ -136,9 +149,7 @@
     query_first = ctx_place * shard_rows
     earlier = passed_along(query_local[shard_rows - row_lead :], "ctx", 1)
     query_ext = jnp.concatenate([earlier, query_local], axis=0)
-    key_all, value_all = lax.all_gather(
-        jnp.stack([key_local, value_local]), "ctx", axis=1, tiled=True
-    )
+    key_all, value_all = ring_gather(jnp.stack([key_local, value_local]), "ctx", 1)
     seq_len = key_all.shape[0]
     key_pad = jnp.concatenate([jnp.zeros((col_lead, width), key_all.dtype), key_all], axis=0)
     key_windows = jnp.stack(

time: 158 us -> 154 us (0.975)
  blocking collectives: 28.5 us -> 8.81 us
  starting transfers between devices: 1.29 us -> 16 us
  between operations: 14.5 us -> 1.34 us
  local copies, waits for them, and re-layouts: 52.8 us -> 60.3 us
  waiting for transfers between devices: 12.6 us -> 18.1 us
    all_to_all x1 -> x0, blocking collectives: 17.8 us -> none  [shards(): lax.all_to_all(stacked, 'uly', split_axis=2, concat_axis=1, tiled=True)]
    all_gather x1 -> x0, waiting for transfers between devices: 12.5 us -> none  [shards(): lax.all_gather(jnp.stack([key_local, value_local]), 'ctx', axis=1, tiled=...]
    ppermute x0 -> x7, waiting for transfers between devices: none -> 10.2 us  [the longest x4 6.45 us: ring_gather(): earlier.append(lax.ppermute(earlier[-1], axis, up))]
    ppermute x0 -> x7, starting transfers between devices: none -> 8.4 us  [the longest x3 7.97 us: ring_gather(): later.append(lax.ppermute(later[-1], axis, down))]
    all_to_all x0 -> x1, waiting for transfers between devices: none -> 7.91 us  [shards(): lax.all_to_all(stacked, 'uly', split_axis=2, concat_axis=1, tiled=True)]
    all_to_all x0 -> x1, starting transfers between devices: none -> 6.32 us  [shards(): lax.all_to_all(stacked, 'uly', split_axis=2, concat_axis=1, tiled=True)]
    unnamed x121 -> x162, local copies, waits for them, and re-layouts: 14.7 us -> 18.5 us
    another operation x7, local copies, waits for them, and re-layouts: 0.75 us -> 3.14 us  [shards(): jnp.stack([query_heads[row_lead - lag:row_lead - lag + shard_rows] for la...]
  transfers between devices with their start and end apart: 2 -> 9, of which waited for: 2 -> 4; matrix products, arithmetic and copies ran while one was open for 8% -> 13% of each run, Pallas kernels for 0% -> 0%
where the time goes in v1:
time: 154 us; the launch traced here: 153 us
  local copies, waits for them, and re-layouts  60.3 us (39%)
  matrix products  38.1 us (25%)
  waiting for transfers between devices  18.1 us (12%)
  starting transfers between devices  16 us (10%)
  other arithmetic  10.3 us (7%)
  blocking collectives  8.81 us (6%)
    unnamed x162, local copies, waits for them, and re-layouts  18.5 us
    another operation x9, local copies, waits for them, and re-layouts, shards(): jnp.stack([key_pad[start:start + KEY_BLOCK + col_lead] for start in range...  14.4 us
    dot_general x1, matrix products, group_logits(): jnp.einsum('ihad,nhard->hinr', shifted, keys_low, preferred_element_type=...  10.9 us
    dot_general x1, matrix products, group_logits(): jnp.einsum('ihad,nhard->hinr', shifted, keys_high, preferred_element_type...  10.4 us
    all_to_all x1, blocking collectives, shards(): lax.all_to_all(attended, 'uly', split_axis=0, concat_axis=1, tiled=True)  8.81 us
    dot_general x1, matrix products, convolved_keys(): jnp.einsum('harc,nchd->nhard', high, key_heads, preferred_element_type=jn...  8.66 us
    ppermute x3, starting transfers between devices, ring_gather(): later.append(lax.ppermute(later[-1], axis, down))  7.97 us
    all_to_all x1, waiting for transfers between devices, shards(): lax.all_to_all(stacked, 'uly', split_axis=2, concat_axis=1, tiled=True)  7.91 us
  transfers between devices with their start and end apart: 9, of which 4 were waited for; matrix products, arithmetic and copies ran while one was open for 13% of the time, Pallas kernels for 0%

profile of v1, /device:TPU:0, one launch (start us, length us, event | category | flops | bytes accessed | tf_op | source)
XLA Modules:
  0.0 152.9 jit_solution(9388925561380246868)
XLA Ops:
  0.0 1.1 pad_maximum_fusion
  1.1 1.4 copy.223
  2.5 2.5 %reshape.295 = bf16[4,2,24576]{2,1,0:T(2,128)(2,1)} reshape(bf16[2048,3,32]{2,1,0:T(4,128)(2,1)S(1)} %bitcast.118) | data formatting | bytes 786432
  4.9 6.3 %all-to-all-start = ((bf16[4,2,24576]{2,1,0:T(2,128)(2,1)}), bf16[4,2,24576]{2,1,0:T(2,128)(2,1)S(1)}, u32[]{:S(2)}, u32[]{:S(2)}) async-start(bf16[4,2,24576]{2,1,0:T(2,128)(2,1)} %reshape.295), calls=%async_computation | async-start | bytes 786432 | tf_op jit(solution)/shard_map/all_to_all | solution.py:139
  11.3 0.8 fusion.129
  12.0 1.0 slice_reduce_fusion.17
  13.0 0.8 fusion.108
  13.8 1.3 fusion.84
  15.0 7.9 %all-to-all-done = bf16[4,2,24576]{2,1,0:T(2,128)(2,1)S(1)} async-done(((bf16[4,2,24576]{2,1,0:T(2,128)(2,1)}), bf16[4,2,24576]{2,1,0:T(2,128)(2,1)S(1)}, u32[]{:S(2)}, u32[]{:S(2)}) %all-to-all-start) | async-done | bytes 393248 | tf_op jit(solution)/shard_map/all_to_all | solution.py:139
  22.9 1.3 reshape.296
  24.3 1.2 copy.282
  25.8 0.7 pad_maximum_fusion.1
  26.5 1.8 %subtract_compare_fusion.5 = (pred[128,8,128]{0,2,1:T(8,128)(4,1)S(1)}, pred[128,8,128]{0,2,1:T(8,128)(4,1)S(1)}, pred[128,8,128]{0,2,1:T(8,128)(4,1)S(1)}, pred...) fusion(s32[8,128]{1,0:T(8,128)S(1)} %multiply_add_fusion, ...), kind=kLoop, calls=%fused_computation.29 | loop fusion | flops 917504 | bytes 791040 | tf_op jit(solution)/shard_map/ge | solution.py:117
  28.4 5.1 %collective-permute-done = bf16[2,128,512]{2,1,0:T(8,128)(2,1)S(1)} collective-permute-done((bf16[2,128,512]{2,1,0:T(8,128)(2,1)}, bf16[2,128,512]{2,1,0:T(8,128)(2,1)S(1)}, u32[]{:S(2)}, u32[]{:S(2)}) %collective-permute-start) | collective-permute-done | bytes 262176 | tf_op jit(solution)/shard_map/ppermute | solution.py:22
  33.4 0.8 slice_reduce_fusion.18
  35.4 0.7 copy.254
  36.1 0.7 copy.253
  37.5 0.7 copy.251
  38.2 0.7 copy.250
  39.5 2.6 %collective-permute-start.4 = (bf16[2,128,512]{2,1,0:T(8,128)(2,1)}, bf16[2,128,512]{2,1,0:T(8,128)(2,1)S(1)}, u32[]{:S(2)}, u32[]{:S(2)}) collective-permute-start(bf16[2,128,512]{2,1,0:T(8,128)(2,1)} %pad_maximum_fusion.1), channel_id=1, source_target_pairs={{0,28},{4,0},{8,4},{12,8},{16,12},{20,16},{24,20},{28,24},{1,29},{... | collective-permute-start | bytes 786440 | tf_op jit(solution)/shard_map/ppermute | solution.py:24
  42.3 1.3 collective-permute-start.7
  44.7 0.8 pad_maximum_fusion.3
  46.2 0.8 copy.238
  47.0 2.6 %collective-permute-start.5 = (bf16[2,128,512]{2,1,0:T(8,128)(2,1)S(1)}, bf16[2,128,512]{2,1,0:T(8,128)(2,1)S(1)}, u32[]{:S(2)}, u32[]{:S(2)}) collective-permute-start(bf16[2,128,512]{2,1,0:T(8,128)(2,1)S(1)} %collective-permute-done.4), channel_id=1, source_target_pairs={{0,28},{4,0},{8,4},{12,8},{16,12},{20,16},{24,20},{28,24},{1,29},{... | collective-permute-start | bytes 786440 | tf_op jit(solution)/shard_map/ppermute | solution.py:24
  49.6 1.4 collective-permute-done.2
  51.0 0.9 constant_dynamic-update-slice_fusion.18
  51.9 0.8 copy.233
  52.7 1.0 copy.239
  53.7 0.8 copy.234
  54.5 1.0 copy.240
  55.5 1.3 concatenate.26
  56.9 2.7 %collective-permute-start.6 = (bf16[2,128,512]{2,1,0:T(8,128)(2,1)S(1)}, bf16[2,128,512]{2,1,0:T(8,128)(2,1)S(1)}, u32[]{:S(2)}, u32[]{:S(2)}) collective-permute-start(bf16[2,128,512]{2,1,0:T(8,128)(2,1)S(1)} %collective-permute-done.5), channel_id=1, source_target_pairs={{0,28},{4,0},{8,4},{12,8},{16,12},{20,16},{24,20},{28,24},{1,29},{... | collective-permute-start | bytes 786440 | tf_op jit(solution)/shard_map/ppermute | solution.py:24
  59.7 3.7 %collective-permute-done.6 = bf16[2,128,512]{2,1,0:T(8,128)(2,1)S(1)} collective-permute-done((bf16[2,128,512]{2,1,0:T(8,128)(2,1)S(1)}, bf16[2,128,512]{2,1,0:T(8,128)(2,1)S(1)}, u32[]{:S(2)}, u32[]{:S(2)}) %collective-permute-start.6) | collective-permute-done | bytes 262176 | tf_op jit(solution)/shard_map/ppermute | solution.py:24
  63.9 1.8 %copy-done = bf16[2,2048,512]{2,1,0:T(8,128)(2,1)} copy-done((bf16[2,2048,512]{2,1,0:T(8,128)(2,1)}, bf16[2,2048,512]{2,1,0:T(8,128)(2,1)S(1)}, u32[]{:S(2)}) %copy-start) | copy-done | bytes 4194328
  66.3 1.6 %stack.75 = bf16[1,138,4,128]{3,2,1,0:T(4,128)(2,1)} reshape(bf16[138,512]{1,0:T(8,128)(2,1)} %pad_slice_fusion) | data formatting | bytes 282624 | tf_op jit(solution)/shard_map/stack | solution.py:155
  67.9 1.6 %copy_dynamic-update-slice_fusion.7 = bf16[8,138,4,128]{3,1,0,2:T(8,128)(2,1)} fusion(bf16[1,138,4,128]{3,2,1,0:T(4,128)(2,1)} %stack.75), kind=kLoop, calls=%fused_computation.138 | loop fusion | bytes 288768
  69.5 2.4 %constant_dynamic-slice_fusion.7 = (bf16[1,138,512]{2,1,0:T(8,128)(2,1)}, bf16[1,138,512]{2,1,0:T(8,128)(2,1)}, bf16[1,138,512]{2,1,0:T(8,128)(2,1)}, bf16[1,138...) fusion(bf16[2,2048,512]{2,1,0:T(8,128)(2,1)} %copy-done, ...), kind=kLoop, calls=%fused_computation.188 | loop fusion | bytes 1978396 | tf_op jit(solution)/shard_map/slice | solution.py:156
  72.0 1.6 %stack.76 = bf16[1,138,4,128]{3,2,1,0:T(4,128)(2,1)} reshape(bf16[1,138,512]{2,1,0:T(8,128)(2,1)} %get-tuple-element.35) | data formatting | bytes 282624 | tf_op jit(solution)/shard_map/stack | solution.py:155
  73.6 1.6 %stack.77 = bf16[1,138,4,128]{3,2,1,0:T(4,128)(2,1)} reshape(bf16[1,138,512]{2,1,0:T(8,128)(2,1)} %get-tuple-element.34) | data formatting | bytes 282624 | tf_op jit(solution)/shard_map/stack | solution.py:155
  75.2 1.6 %stack.78 = bf16[1,138,4,128]{3,2,1,0:T(4,128)(2,1)} reshape(bf16[1,138,512]{2,1,0:T(8,128)(2,1)} %get-tuple-element.33) | data formatting | bytes 282624 | tf_op jit(solution)/shard_map/stack | solution.py:155
  76.8 1.6 %stack.79 = bf16[1,138,4,128]{3,2,1,0:T(4,128)(2,1)} reshape(bf16[1,138,512]{2,1,0:T(8,128)(2,1)} %get-tuple-element.32) | data formatting | bytes 282624 | tf_op jit(solution)/shard_map/stack | solution.py:155
  78.4 1.6 %stack.80 = bf16[1,138,4,128]{3,2,1,0:T(4,128)(2,1)} reshape(bf16[1,138,512]{2,1,0:T(8,128)(2,1)} %get-tuple-element.31) | data formatting | bytes 282624 | tf_op jit(solution)/shard_map/stack | solution.py:155
  80.0 1.6 %stack.81 = bf16[1,138,4,128]{3,2,1,0:T(4,128)(2,1)} reshape(bf16[1,138,512]{2,1,0:T(8,128)(2,1)} %get-tuple-element.30) | data formatting | bytes 282624 | tf_op jit(solution)/shard_map/stack | solution.py:155
  81.6 1.6 %stack.82 = bf16[1,138,4,128]{3,2,1,0:T(4,128)(2,1)} reshape(bf16[1,138,512]{2,1,0:T(8,128)(2,1)} %get-tuple-element.29) | data formatting | bytes 282624 | tf_op jit(solution)/shard_map/stack | solution.py:155
  83.2 1.6 %copy_dynamic-update-slice_fusion.6 = bf16[8,138,4,128]{3,1,0,2:T(8,128)(2,1)} fusion(bf16[8,138,4,128]{3,1,0,2:T(8,128)(2,1)} %copy_dynamic-update-slice_fusion.7, bf16[1,138,4,128]{3,2,1,0:T(4,128)(2,1)} %stack.76), kind=kLoop, calls=%fused_computation.137 | loop fusion | bytes 288768
  84.8 1.6 %copy_dynamic-update-slice_fusion.5 = bf16[8,138,4,128]{3,1,0,2:T(8,128)(2,1)} fusion(bf16[8,138,4,128]{3,1,0,2:T(8,128)(2,1)} %copy_dynamic-update-slice_fusion.6, bf16[1,138,4,128]{3,2,1,0:T(4,128)(2,1)} %stack.77), kind=kLoop, calls=%fused_computation.136 | loop fusion | bytes 288768
  86.3 1.6 %copy_dynamic-update-slice_fusion.4 = bf16[8,138,4,128]{3,1,0,2:T(8,128)(2,1)} fusion(bf16[8,138,4,128]{3,1,0,2:T(8,128)(2,1)} %copy_dynamic-update-slice_fusion.5, bf16[1,138,4,128]{3,2,1,0:T(4,128)(2,1)} %stack.78), kind=kLoop, calls=%fused_computation.135 | loop fusion | bytes 288768
  87.9 1.6 %copy_dynamic-update-slice_fusion.3 = bf16[8,138,4,128]{3,1,0,2:T(8,128)(2,1)} fusion(bf16[8,138,4,128]{3,1,0,2:T(8,128)(2,1)} %copy_dynamic-update-slice_fusion.4, bf16[1,138,4,128]{3,2,1,0:T(4,128)(2,1)} %stack.79), kind=kLoop, calls=%fused_computation.134 | loop fusion | bytes 288768
  89.5 1.6 %copy_dynamic-update-slice_fusion.2 = bf16[8,138,4,128]{3,1,0,2:T(8,128)(2,1)} fusion(bf16[8,138,4,128]{3,1,0,2:T(8,128)(2,1)} %copy_dynamic-update-slice_fusion.3, bf16[1,138,4,128]{3,2,1,0:T(4,128)(2,1)} %stack.80), kind=kLoop, calls=%fused_computation.133 | loop fusion | bytes 288768
  91.1 1.6 %copy_dynamic-update-slice_fusion.1 = bf16[8,138,4,128]{3,1,0,2:T(8,128)(2,1)} fusion(bf16[8,138,4,128]{3,1,0,2:T(8,128)(2,1)} %copy_dynamic-update-slice_fusion.2, bf16[1,138,4,128]{3,2,1,0:T(4,128)(2,1)} %stack.81), kind=kLoop, calls=%fused_computation.132 | loop fusion | bytes 288768
  92.7 1.6 %copy_dynamic-update-slice_fusion = bf16[8,138,4,128]{3,1,0,2:T(8,128)(2,1)} fusion(bf16[8,138,4,128]{3,1,0,2:T(8,128)(2,1)} %copy_dynamic-update-slice_fusion.1, bf16[1,138,4,128]{3,2,1,0:T(4,128)(2,1)} %stack.82), kind=kLoop, calls=%fused_computation.131 | loop fusion | bytes 288768 | tf_op jit(solution)/shard_map/stack | solution.py:155
  94.4 8.7 %fusion.17 = f32[4,8,128,6,128]{4,2,3,1,0:T(8,128)} fusion(bf16[8,138,4,128]{3,1,0,2:T(8,128)(2,1)} %copy_dynamic-update-slice_fusion, f32[4,6]{1,0:T(4,128)S(1)} %bitcast.139, f32[4,6]{1,0:T(4,128)S(1)} %bitcast.141, f32[4,6]{1,0:T(4,128)S(1)} %bitcast.143, f32[4,6]{1,0:T(4,128)S(1)} %bitcast.145, f32[4,6]{1,0:T(4,128)} %bitcast.147, ...), kind=kOutput, calls=%fused_computation.32 | convolution fusion | flops 873732096 | bytes 13908768 | tf_op jit(solution)/shard_map/harc,nchd->nhard/dot_general | solution.py:59
  103.3 6.3 %fusion.15 = f32[4,8,128,6,128]{4,2,3,1,0:T(8,128)} fusion(bf16[8,138,4,128]{3,1,0,2:T(8,128)(2,1)S(1)} %copy-done.1, f32[4,6]{1,0:T(4,128)S(1)} %bitcast.140, f32[4,6]{1,0:T(4,128)S(1)} %bitcast.142, f32[4,6]{1,0:T(4,128)S(1)} %bitcast.144, f32[4,6]{1,0:T(4,128)S(1)} %bitcast.146, f32[4,6]{1,0:T(4,128)S(1)} %bitcast.148, f32[4,6]{1,0:T(4,128)S(1)} %bitcast.150, ...), kind=kOutput, calls=%fused_computation.30 | convolution fusion | flops 874156032 | bytes 13908768 | tf_op jit(solution)/shard_map/harc,nchd->nhard/dot_general | solution.py:61
  109.6 1.4 copy.227
  111.9 0.8 fusion.90
  113.3 10.9 %fusion.1 = f32[4,128,8,128,1]{1,3,4,2,0:T(8,128)S(1)} fusion(f32[4,8,128,6,128]{4,2,3,1,0:T(8,128)} %fusion.17, f32[4,8,128,6,128]{4,2,3,1,0:T(8,128)} %fusion.15, bf16[128,4,6,128]{3,0,2,1:T(8,128)(2,1)S(1)} %constant_dynamic-update-slice_fusion.16), kind=kOutput, calls=%fused_computation.3 | convolution fusion | flops 817889280 | bytes 28049408 | tf_op jit(solution)/shard_map/ihad,nhard->hinr/dot_general | solution.py:97
  124.6 10.4 %fusion.85 = (f32[4,128]{1,0:T(4,128)S(1)}, f32[4,128,8,128]{1,3,2,0:T(8,128)S(1)}) fusion(f32[4,128]{1,0:T(4,128)S(1)} %get-tuple-element.74, pred[128,8,128]{0,2,1:T(8,128)(4,1)S(1)} %get-tuple-element.69, f32[4,128]{1,0:T(4,128)S(1)} %get-tuple-element.67, pred[128,8,128]{0,2,1:T(8,128)(4,1)S(1)} %get-tuple-element.70, ...), kind=kOutput, calls=%fused_computation.115 | convolution fusion | flops 821558784 | bytes 30945280 | tf_op jit(solution)/shard_map/ihad,nhard->hinr/dot_general | solution.py:95
  135.1 1.3 exponential_reduce_fusion
  136.4 1.3 fusion.13
  137.9 1.0 copy.271
  138.9 1.0 copy.270
  139.9 1.0 copy.269
  141.2 1.8 %multiply_reduce_fusion = (f32[128,4]{0,1:T(4,128)S(1)}, f32[128,4,128]{0,2,1:T(8,128)S(1)}) fusion(bf16[1024,4,128]{0,2,1:T(8,128)(2,1)S(1)} %bitcast.129, f32[128,1024]{1,0:T(8,128)S(1)} %copy-done.5, f32[4]{0:T(128)S(1)} %copy-done.64, f32[128,1024]{1,0:T(8,128)S(1)} %copy-done.6, f32[4]{0:T(128)S(1)} %copy-done.65, f32[128,1024]{1,0:T(8,128)} %copy.269, ...), kind=kOutput, calls=%fused_computation.127 | convolution fusion | flops 138542592 | bytes 3409984 | tf_op jit(solution)/shard_map/hik,khd->ihd/dot_general | solution.py:127
  143.4 8.8 %all_to_all.34 = bf16[4,32,512]{2,1,0:T(8,128)(2,1)S(1)} all-to-all(bf16[4,32,512]{2,1,0:T(8,128)(2,1)S(1)} %all_to_all.28), channel_id=1, replica_groups=mesh['ctx'=8,'uly'=4] {'uly'}, dimensions={0} | all-to-all | bytes 262144 | tf_op jit(solution)/shard_map/all_to_all | solution.py:191
  (214 shorter events, 9.0 us)
Async XLA Ops:
  2.4 8.8 %copy-start.25 = (f32[4,6,11]{2,0,1:T(4,128)S(1)}, f32[4,6,11]{2,0,1:T(4,128)}, u32[]{:S(2)}) copy-start(f32[4,6,11]{2,0,1:T(4,128)} %param.9) | copy-start | bytes 3172
  4.9 18.0 %all-to-all-start = ((bf16[4,2,24576]{2,1,0:T(2,128)(2,1)}), bf16[4,2,24576]{2,1,0:T(2,128)(2,1)S(1)}, u32[]{:S(2)}, u32[]{:S(2)}) async-start(bf16[4,2,24576]{2,1,0:T(2,128)(2,1)} %reshape.295), calls=%async_computation | async-start | bytes 786432 | tf_op jit(solution)/shard_map/all_to_all | solution.py:139
  12.0 13.5 %copy-start.62 = (s32[128]{0:T(128)}, s32[128]{0:T(128)S(1)}, u32[]{:S(2)}) copy-start(s32[128]{0:T(128)S(1)} %iota_add_fusion.1) | copy-start | bytes 1540
  24.3 9.2 %copy-start.44 = (f32[4,4]{1,0:T(4,128)S(1)}, f32[4,4]{1,0:T(4,128)}, u32[]{:S(2)}) copy-start(f32[4,4]{1,0:T(4,128)} %param.10) | copy-start | bytes 196
  25.5 8.9 %copy-start.42 = (f32[4,6,1]{2,0,1:T(4,128)S(1)}, f32[4,6,1]{2,0,1:T(4,128)}, u32[]{:S(2)}) copy-start(f32[4,6,1]{2,0,1:T(4,128)} %get-tuple-element.57) | copy-start | bytes 292
  25.5 9.0 %copy-start.41 = (f32[4,6,1]{2,0,1:T(4,128)S(1)}, f32[4,6,1]{2,0,1:T(4,128)}, u32[]{:S(2)}) copy-start(f32[4,6,1]{2,0,1:T(4,128)} %get-tuple-element.58) | copy-start | bytes 292
  25.5 9.1 %copy-start.40 = (f32[4,6,1]{2,0,1:T(4,128)S(1)}, f32[4,6,1]{2,0,1:T(4,128)}, u32[]{:S(2)}) copy-start(f32[4,6,1]{2,0,1:T(4,128)} %get-tuple-element.59) | copy-start | bytes 292
  25.5 9.2 %copy-start.39 = (f32[4,6,1]{2,0,1:T(4,128)S(1)}, f32[4,6,1]{2,0,1:T(4,128)}, u32[]{:S(2)}) copy-start(f32[4,6,1]{2,0,1:T(4,128)} %get-tuple-element.60) | copy-start | bytes 292
  25.5 9.9 %copy-start.38 = (f32[4,6,1]{2,0,1:T(4,128)S(1)}, f32[4,6,1]{2,0,1:T(4,128)}, u32[]{:S(2)}) copy-start(f32[4,6,1]{2,0,1:T(4,128)} %get-tuple-element.61) | copy-start | bytes 292
  25.5 10.6 %copy-start.37 = (f32[4,6,1]{2,0,1:T(4,128)S(1)}, f32[4,6,1]{2,0,1:T(4,128)}, u32[]{:S(2)}) copy-start(f32[4,6,1]{2,0,1:T(4,128)} %get-tuple-element.62) | copy-start | bytes 292
  25.5 11.2 %copy-start.36 = (f32[4,6,1]{2,0,1:T(4,128)S(1)}, f32[4,6,1]{2,0,1:T(4,128)}, u32[]{:S(2)}) copy-start(f32[4,6,1]{2,0,1:T(4,128)} %get-tuple-element.63) | copy-start | bytes 292
  25.6 11.9 %copy-start.35 = (f32[4,6,1]{2,0,1:T(4,128)S(1)}, f32[4,6,1]{2,0,1:T(4,128)}, u32[]{:S(2)}) copy-start(f32[4,6,1]{2,0,1:T(4,128)} %get-tuple-element.64) | copy-start | bytes 292
  25.6 12.6 %copy-start.34 = (f32[4,6,1]{2,0,1:T(4,128)S(1)}, f32[4,6,1]{2,0,1:T(4,128)}, u32[]{:S(2)}) copy-start(f32[4,6,1]{2,0,1:T(4,128)} %get-tuple-element.65) | copy-start | bytes 292
  25.6 13.3 %copy-start.33 = (f32[4,6,1]{2,0,1:T(4,128)S(1)}, f32[4,6,1]{2,0,1:T(4,128)}, u32[]{:S(2)}) copy-start(f32[4,6,1]{2,0,1:T(4,128)} %get-tuple-element.55) | copy-start | bytes 292
  26.5 6.9 %collective-permute-start = (bf16[2,128,512]{2,1,0:T(8,128)(2,1)}, bf16[2,128,512]{2,1,0:T(8,128)(2,1)S(1)}, u32[]{:S(2)}, u32[]{:S(2)}) collective-permute-start(bf16[2,128,512]{2,1,0:T(8,128)(2,1)} %pad_maximum_fusion.1), channel_id=1, source_target_pairs={{0,4},{4,8},{8,12},{12,16},{16,20},{20,24},{24,28},{28,0},{1,5},{5... | collective-permute-start | bytes 786440 | tf_op jit(solution)/shard_map/ppermute | solution.py:22
  33.4 10.8 %collective-permute-start.1 = (bf16[2,128,512]{2,1,0:T(8,128)(2,1)S(1)}, bf16[2,128,512]{2,1,0:T(8,128)(2,1)S(1)}, u32[]{:S(2)}, u32[]{:S(2)}) collective-permute-start(bf16[2,128,512]{2,1,0:T(8,128)(2,1)S(1)} %collective-permute-done), channel_id=1, source_target_pairs={{0,4},{4,8},{8,12},{12,16},{16,20},{20,24},{24,28},{28,0},{1,5},{5... | collective-permute-start | bytes 786440 | tf_op jit(solution)/shard_map/ppermute | solution.py:22
  39.5 7.4 %collective-permute-start.4 = (bf16[2,128,512]{2,1,0:T(8,128)(2,1)}, bf16[2,128,512]{2,1,0:T(8,128)(2,1)S(1)}, u32[]{:S(2)}, u32[]{:S(2)}) collective-permute-start(bf16[2,128,512]{2,1,0:T(8,128)(2,1)} %pad_maximum_fusion.1), channel_id=1, source_target_pairs={{0,28},{4,0},{8,4},{12,8},{16,12},{20,16},{24,20},{28,24},{1,29},{... | collective-permute-start | bytes 786440 | tf_op jit(solution)/shard_map/ppermute | solution.py:24
  42.3 2.5 %collective-permute-start.7 = (bf16[5,512]{1,0:T(8,128)(2,1)S(1)}, bf16[5,512]{1,0:T(8,128)(2,1)S(1)}, u32[]{:S(2)}, u32[]{:S(2)}) collective-permute-start(bf16[5,512]{1,0:T(8,128)(2,1)S(1)} %slice.356), channel_id=1, source_target_pairs={{0,4},{4,8},{8,12},{12,16},{16,20},{20,24},{24,28},{1,5},{5,9},{9,... | collective-permute-start | bytes 15368 | tf_op jit(solution)/shard_map/ppermute | solution.py:32
  44.3 6.7 %collective-permute-start.2 = (bf16[2,128,512]{2,1,0:T(8,128)(2,1)S(1)}, bf16[2,128,512]{2,1,0:T(8,128)(2,1)S(1)}, u32[]{:S(2)}, u32[]{:S(2)}) collective-permute-start(bf16[2,128,512]{2,1,0:T(8,128)(2,1)S(1)} %collective-permute-done.1), channel_id=1, source_target_pairs={{0,4},{4,8},{8,12},{12,16},{16,20},{20,24},{24,28},{28,0},{1,5},{5... | collective-permute-start | bytes 786440 | tf_op jit(solution)/shard_map/ppermute | solution.py:22
  45.5 6.4 %copy-start.4 = (bf16[128,512]{1,0:T(8,128)(2,1)S(1)}, bf16[128,512]{1,0:T(8,128)(2,1)}, u32[]{:S(2)}) copy-start(bf16[128,512]{1,0:T(8,128)(2,1)} %get-tuple-element.54) | copy-start | bytes 393220
  47.0 9.9 %collective-permute-start.5 = (bf16[2,128,512]{2,1,0:T(8,128)(2,1)S(1)}, bf16[2,128,512]{2,1,0:T(8,128)(2,1)S(1)}, u32[]{:S(2)}, u32[]{:S(2)}) collective-permute-start(bf16[2,128,512]{2,1,0:T(8,128)(2,1)S(1)} %collective-permute-done.4), channel_id=1, source_target_pairs={{0,28},{4,0},{8,4},{12,8},{16,12},{20,16},{24,20},{28,24},{1,29},{... | collective-permute-start | bytes 786440 | tf_op jit(solution)/shard_map/ppermute | solution.py:24
  51.0 8.6 %collective-permute-start.3 = (bf16[2,128,512]{2,1,0:T(8,128)(2,1)S(1)}, bf16[2,128,512]{2,1,0:T(8,128)(2,1)S(1)}, u32[]{:S(2)}, u32[]{:S(2)}) collective-permute-start(bf16[2,128,512]{2,1,0:T(8,128)(2,1)S(1)} %collective-permute-done.2), channel_id=1, source_target_pairs={{0,4},{4,8},{8,12},{12,16},{16,20},{20,24},{24,28},{28,0},{1,5},{5... | collective-permute-start | bytes 786440 | tf_op jit(solution)/shard_map/ppermute | solution.py:22
  56.9 6.6 %collective-permute-start.6 = (bf16[2,128,512]{2,1,0:T(8,128)(2,1)S(1)}, bf16[2,128,512]{2,1,0:T(8,128)(2,1)S(1)}, u32[]{:S(2)}, u32[]{:S(2)}) collective-permute-start(bf16[2,128,512]{2,1,0:T(8,128)(2,1)S(1)} %collective-permute-done.5), channel_id=1, source_target_pairs={{0,28},{4,0},{8,4},{12,8},{16,12},{20,16},{24,20},{28,24},{1,29},{... | collective-permute-start | bytes 786440 | tf_op jit(solution)/shard_map/ppermute | solution.py:24
  94.3 8.8 %copy-start.1 = (bf16[8,138,4,128]{3,1,0,2:T(8,128)(2,1)S(1)}, bf16[8,138,4,128]{3,1,0,2:T(8,128)(2,1)}, u32[]{:S(2)}) copy-start(bf16[8,138,4,128]{3,1,0,2:T(8,128)(2,1)} %copy_dynamic-update-slice_fusion) | copy-start | bytes 3391492
  94.3 8.8 %copy-start.14 = (pred[128,138]{0,1:T(8,128)(4,1)S(1)}, pred[128,138]{0,1:T(8,128)(4,1)}, u32[]{:S(2)}) copy-start(pred[128,138]{0,1:T(8,128)(4,1)} %get-tuple-element.81) | copy-start | bytes 52996
  94.3 8.8 %copy-start.15 = (pred[128,138]{0,1:T(8,128)(4,1)S(1)}, pred[128,138]{0,1:T(8,128)(4,1)}, u32[]{:S(2)}) copy-start(pred[128,138]{0,1:T(8,128)(4,1)} %get-tuple-element.82) | copy-start | bytes 52996
  94.3 8.8 %copy-start.16 = (pred[128,138]{0,1:T(8,128)(4,1)S(1)}, pred[128,138]{0,1:T(8,128)(4,1)}, u32[]{:S(2)}) copy-start(pred[128,138]{0,1:T(8,128)(4,1)} %get-tuple-element.83) | copy-start | bytes 52996
  94.3 8.8 %copy-start.17 = (pred[128,138]{0,1:T(8,128)(4,1)S(1)}, pred[128,138]{0,1:T(8,128)(4,1)}, u32[]{:S(2)}) copy-start(pred[128,138]{0,1:T(8,128)(4,1)} %get-tuple-element.84) | copy-start | bytes 52996
  94.3 8.8 %copy-start.18 = (pred[128,138]{0,1:T(8,128)(4,1)S(1)}, pred[128,138]{0,1:T(8,128)(4,1)}, u32[]{:S(2)}) copy-start(pred[128,138]{0,1:T(8,128)(4,1)} %get-tuple-element.85) | copy-start | bytes 52996
  94.3 8.8 %copy-start.19 = (pred[128,138]{0,1:T(8,128)(4,1)S(1)}, pred[128,138]{0,1:T(8,128)(4,1)}, u32[]{:S(2)}) copy-start(pred[128,138]{0,1:T(8,128)(4,1)} %get-tuple-element.86) | copy-start | bytes 52996
  94.3 8.8 %copy-start.20 = (pred[128,138]{0,1:T(8,128)(4,1)S(1)}, pred[128,138]{0,1:T(8,128)(4,1)}, u32[]{:S(2)}) copy-start(pred[128,138]{0,1:T(8,128)(4,1)} %get-tuple-element.87) | copy-start | bytes 52996
  94.3 8.8 %copy-start.21 = (pred[128,138]{0,1:T(8,128)(4,1)S(1)}, pred[128,138]{0,1:T(8,128)(4,1)}, u32[]{:S(2)}) copy-start(pred[128,138]{0,1:T(8,128)(4,1)} %get-tuple-element.88) | copy-start | bytes 52996
  94.3 8.8 %copy-start.22 = (pred[128,138]{0,1:T(8,128)(4,1)S(1)}, pred[128,138]{0,1:T(8,128)(4,1)}, u32[]{:S(2)}) copy-start(pred[128,138]{0,1:T(8,128)(4,1)} %get-tuple-element.89) | copy-start | bytes 52996
  94.4 8.8 %copy-start.23 = (pred[128,138]{0,1:T(8,128)(4,1)S(1)}, pred[128,138]{0,1:T(8,128)(4,1)}, u32[]{:S(2)}) copy-start(pred[128,138]{0,1:T(8,128)(4,1)} %get-tuple-element.90) | copy-start | bytes 52996
  94.4 8.8 %copy-start.24 = (pred[128,138]{0,1:T(8,128)(4,1)S(1)}, pred[128,138]{0,1:T(8,128)(4,1)}, u32[]{:S(2)}) copy-start(pred[128,138]{0,1:T(8,128)(4,1)} %get-tuple-element.91) | copy-start | bytes 52996
  94.4 8.8 %copy-start.26 = (f32[4,6,1]{1,0,2:T(4,128)S(1)}, f32[4,6,1]{1,0,2:T(4,128)}, u32[]{:S(2)}) copy-start(f32[4,6,1]{1,0,2:T(4,128)} %copy.255) | copy-start | bytes 292
  94.4 8.8 %copy-start.27 = (f32[4,6,1]{1,0,2:T(4,128)S(1)}, f32[4,6,1]{1,0,2:T(4,128)}, u32[]{:S(2)}) copy-start(f32[4,6,1]{1,0,2:T(4,128)} %copy.254) | copy-start | bytes 292
  94.4 8.8 %copy-start.28 = (f32[4,6,1]{1,0,2:T(4,128)S(1)}, f32[4,6,1]{1,0,2:T(4,128)}, u32[]{:S(2)}) copy-start(f32[4,6,1]{1,0,2:T(4,128)} %copy.253) | copy-start | bytes 292
  94.4 8.8 %copy-start.29 = (f32[4,6,1]{1,0,2:T(4,128)S(1)}, f32[4,6,1]{1,0,2:T(4,128)}, u32[]{:S(2)}) copy-start(f32[4,6,1]{1,0,2:T(4,128)} %copy.252) | copy-start | bytes 292
  94.4 8.8 %copy-start.30 = (f32[4,6,1]{1,0,2:T(4,128)S(1)}, f32[4,6,1]{1,0,2:T(4,128)}, u32[]{:S(2)}) copy-start(f32[4,6,1]{1,0,2:T(4,128)} %copy.251) | copy-start | bytes 292
  94.4 8.8 %copy-start.31 = (f32[4,6,1]{1,0,2:T(4,128)S(1)}, f32[4,6,1]{1,0,2:T(4,128)}, u32[]{:S(2)}) copy-start(f32[4,6,1]{1,0,2:T(4,128)} %copy.250) | copy-start | bytes 292
  94.4 8.8 %copy-start.32 = (f32[4,6,1]{1,0,2:T(4,128)S(1)}, f32[4,6,1]{1,0,2:T(4,128)}, u32[]{:S(2)}) copy-start(f32[4,6,1]{1,0,2:T(4,128)} %copy.249) | copy-start | bytes 292
  113.2 11.0 %copy-start.46 = (f32[4]{0:T(128)S(1)}, f32[4]{0:T(128)}, u32[]{:S(2)}) copy-start(f32[4]{0:T(128)} %get-tuple-element.11) | copy-start | bytes 52
  113.2 11.0 %copy-start.47 = (f32[4]{0:T(128)S(1)}, f32[4]{0:T(128)}, u32[]{:S(2)}) copy-start(f32[4]{0:T(128)} %get-tuple-element.12) | copy-start | bytes 52
  113.2 11.0 %copy-start.48 = (f32[4]{0:T(128)S(1)}, f32[4]{0:T(128)}, u32[]{:S(2)}) copy-start(f32[4]{0:T(128)} %get-tuple-element.13) | copy-start | bytes 52
  113.2 11.0 %copy-start.49 = (f32[4]{0:T(128)S(1)}, f32[4]{0:T(128)}, u32[]{:S(2)}) copy-start(f32[4]{0:T(128)} %get-tuple-element.16) | copy-start | bytes 52
  113.2 11.0 %copy-start.50 = (f32[4]{0:T(128)S(1)}, f32[4]{0:T(128)}, u32[]{:S(2)}) copy-start(f32[4]{0:T(128)} %get-tuple-element.17) | copy-start | bytes 52
  113.2 11.0 %copy-start.51 = (f32[4]{0:T(128)S(1)}, f32[4]{0:T(128)}, u32[]{:S(2)}) copy-start(f32[4]{0:T(128)} %get-tuple-element.20) | copy-start | bytes 52
  113.2 11.1 %copy-start.52 = (f32[4]{0:T(128)S(1)}, f32[4]{0:T(128)}, u32[]{:S(2)}) copy-start(f32[4]{0:T(128)} %get-tuple-element.15) | copy-start | bytes 52
  113.2 11.1 %copy-start.53 = (f32[4]{0:T(128)S(1)}, f32[4]{0:T(128)}, u32[]{:S(2)}) copy-start(f32[4]{0:T(128)} %get-tuple-element.19) | copy-start | bytes 52
  113.2 11.1 %copy-start.54 = (f32[4]{0:T(128)S(1)}, f32[4]{0:T(128)}, u32[]{:S(2)}) copy-start(f32[4]{0:T(128)} %get-tuple-element.22) | copy-start | bytes 52
  113.3 11.1 %copy-start.55 = (f32[4]{0:T(128)S(1)}, f32[4]{0:T(128)}, u32[]{:S(2)}) copy-start(f32[4]{0:T(128)} %get-tuple-element.24) | copy-start | bytes 52
  113.3 11.2 %copy-start.57 = (f32[4]{0:T(128)S(1)}, f32[4]{0:T(128)}, u32[]{:S(2)}) copy-start(f32[4]{0:T(128)} %get-tuple-element.10) | copy-start | bytes 52
  113.3 11.2 %copy-start.58 = (f32[4]{0:T(128)S(1)}, f32[4]{0:T(128)}, u32[]{:S(2)}) copy-start(f32[4]{0:T(128)} %get-tuple-element.14) | copy-start | bytes 52
  113.3 11.2 %copy-start.59 = (f32[4]{0:T(128)S(1)}, f32[4]{0:T(128)}, u32[]{:S(2)}) copy-start(f32[4]{0:T(128)} %get-tuple-element.18) | copy-start | bytes 52
  113.3 11.2 %copy-start.60 = (f32[4]{0:T(128)S(1)}, f32[4]{0:T(128)}, u32[]{:S(2)}) copy-start(f32[4]{0:T(128)} %get-tuple-element.21) | copy-start | bytes 52
  113.3 11.2 %copy-start.61 = (f32[4]{0:T(128)S(1)}, f32[4]{0:T(128)}, u32[]{:S(2)}) copy-start(f32[4]{0:T(128)} %get-tuple-element.23) | copy-start | bytes 52
  113.3 11.3 %copy-start.2 = (pred[128,8,128]{0,2,1:T(8,128)(4,1)S(1)}, pred[128,8,128]{0,2,1:T(8,128)(4,1)}, u32[]{:S(2)}) copy-start(pred[128,8,128]{0,2,1:T(8,128)(4,1)} %get-tuple-element.73) | copy-start | bytes 393220
  137.8 3.3 %copy-start.3 = (bf16[1,1024,512]{1,2,0:T(8,128)(2,1)S(1)}, bf16[1,1024,512]{1,2,0:T(8,128)(2,1)}, u32[]{:S(2)}) copy-start(bf16[1,1024,512]{1,2,0:T(8,128)(2,1)} %copy.227) | copy-start | bytes 3145732
  137.8 3.3 %copy-start.63 = (f32[4]{0:T(128)S(1)}, f32[4]{0:T(128)}, u32[]{:S(2)}) copy-start(f32[4]{0:T(128)} %get-tuple-element.25) | copy-start | bytes 52
  137.9 3.3 %copy-start.64 = (f32[4]{0:T(128)S(1)}, f32[4]{0:T(128)}, u32[]{:S(2)}) copy-start(f32[4]{0:T(128)} %get-tuple-element.26) | copy-start | bytes 52
  137.9 3.3 %copy-start.65 = (f32[4]{0:T(128)S(1)}, f32[4]{0:T(128)}, u32[]{:S(2)}) copy-start(f32[4]{0:T(128)} %get-tuple-element.27) | copy-start | bytes 52
  137.9 3.3 %copy-start.66 = (f32[4]{0:T(128)S(1)}, f32[4]{0:T(128)}, u32[]{:S(2)}) copy-start(f32[4]{0:T(128)} %get-tuple-element.28) | copy-start | bytes 52
  138.9 2.3 %copy-start.5 = (f32[128,1024]{1,0:T(8,128)S(1)}, f32[128,1024]{1,0:T(8,128)}, u32[]{:S(2)}) copy-start(f32[128,1024]{1,0:T(8,128)} %copy.271) | copy-start | bytes 1572868
  (12 other events, 15.6 us)
